TPU v7x, 512 devices: a whole 4x4x16 slice. The times are simulated.
512 devices in a mesh: template: 16 (over y, x_hi, core), fsdp: 16 (over z), dp: 2 (over x_lo).
Axes of the slice: x: 4 (x_hi: 2, x_lo: 2; x = x_hi * 2 + x_lo), y: 4, z: 16, core: 2. Of those that a mesh axis runs over, the one named last changes fastest.
Arguments:
- hidden: bfloat16 [16, 4096, 8192], P('template', ('fsdp', 'dp')), may hold values from -6 to 6
- target: bfloat16 [16, 4096, 512], P('template', ('fsdp', 'dp')), may hold values from -6 to 6
- weight: bfloat16 [16, 8192, 512], P('template', 'fsdp'), may hold values from -6 to 6
- gain: bfloat16 [16, 8192], P('template', 'fsdp'), may hold values from 0.099609375 to 1.8984375
Outputs:
- merged_weight: float32 [8192, 512], P(('fsdp', 'dp'))
- merged_gain: float32 [8192], P(('fsdp', 'dp'))
All inputs are finite; a program needn't handle non-finite values.
Results may differ from a plain program's by a relative error of at most 0.0018.
Values may be sent and summed in bfloat16 or wider, within the bound.
No kernel may reach another device: no remote copies, remote signals or barrier semaphores. Data moves between devices by JAX's collectives and lax.ppermute only.
A program may use at most 64 MiB of HBM per device.

v0:
```python
import math
import jax
import jax.numpy as jnp
from jax import lax
from jax.sharding import PartitionSpec as P


def body(hidden, target, weight, gain):
    token_batch = hidden[0]
    goal = target[0]
    w_shard = weight[0]
    g_shard = gain[0]
    width = token_batch.shape[1]
    rows = w_shard.shape[0]
    heads = w_shard.shape[1]
    scale = 1.0 / math.sqrt(width)
    n_t = lax.axis_size("template")
    n_dp = lax.axis_size("dp")
    hidden_f = token_batch.astype(jnp.float32)
    ratio = lax.rsqrt(jnp.mean(jnp.square(hidden_f), axis=1, keepdims=True) + 1e-05)
    swap = [(i, (i + 1) % n_dp) for i in range(n_dp)]
    other_hidden = lax.ppermute(token_batch, "dp", swap)
    other_f = other_hidden.astype(jnp.float32)
    other_ratio = lax.rsqrt(jnp.mean(jnp.square(other_f), axis=1, keepdims=True) + 1e-05)
    half = heads // n_dp
    dp_at = lax.axis_index("dp")
    w_cols = lax.dynamic_slice_in_dim(w_shard, dp_at * half, half, 1)
    w_ext = jnp.concatenate([w_cols, g_shard.reshape(-1, half)], axis=0)
    gathered = lax.all_gather(w_ext, "fsdp", axis=0, tiled=False)
    w_half = gathered[:, :rows, :]
    g_full = gathered[:, rows:, :].reshape(-1).astype(jnp.float32)
    xhat = hidden_f * ratio
    normed = (xhat * g_full[None, :]).astype(jnp.bfloat16)
    other_normed = (other_f * other_ratio * g_full[None, :]).astype(jnp.bfloat16)
    n_blocks = gathered.shape[0]
    mine_half = jnp.einsum(
        "tfr,frh->th",
        normed.reshape(-1, n_blocks, rows),
        w_half,
        preferred_element_type=jnp.float32,
    )
    theirs_half = jnp.einsum(
        "tfr,frh->th",
        other_normed.reshape(-1, n_blocks, rows),
        w_half,
        preferred_element_type=jnp.float32,
    )
    from_other = lax.ppermute(theirs_half, "dp", swap)
    both = jnp.stack([mine_half, from_other])
    first = jnp.where(dp_at == 0, both[0], both[1])
    second = jnp.where(dp_at == 0, both[1], both[0])
    values = jnp.concatenate([first, second], axis=1) * scale
    delta = (values - goal.astype(jnp.float32)).astype(jnp.bfloat16)
    n_f = lax.axis_size("fsdp")
    by_dest = jnp.transpose(token_batch.reshape(token_batch.shape[0], n_f, rows), (1, 0, 2))
    late_batch, _ = lax.optimization_barrier((by_dest, theirs_half))
    local_hidden = lax.all_to_all(late_batch, "fsdp", 0, 0, tiled=True).reshape(-1, rows)
    local_ratio = lax.all_gather(ratio, "fsdp", axis=0, tiled=True)
    local_delta = lax.all_gather(delta, "fsdp", axis=0, tiled=True)
    local_xhat = local_hidden.astype(jnp.float32) * local_ratio
    g_f = g_shard.astype(jnp.float32)
    local_normed = (local_xhat * g_f[None, :]).astype(jnp.bfloat16)
    sq_normed = jnp.square(local_normed.astype(jnp.float32)).astype(jnp.bfloat16)
    sq_delta = jnp.square(local_delta.astype(jnp.float32)).astype(jnp.bfloat16)
    fisher = jnp.einsum("td,th->dh", sq_normed, sq_delta, preferred_element_type=jnp.float32)
    back = jnp.einsum("th,dh->td", local_delta, w_shard, preferred_element_type=jnp.float32) * scale
    gain_info = jnp.sum(jnp.square(back * local_xhat), axis=0)
    extra = jnp.zeros((rows, 128), jnp.float32)
    extra = extra.at[:, 0].set(gain_info * g_f).at[:, 1].set(gain_info)
    pack = jnp.concatenate([fisher * w_shard.astype(jnp.float32), fisher, extra], axis=1)
    cols = pack.shape[1]
    piece = rows // (n_t * n_dp)
    pack = pack.reshape(n_t * n_dp, piece, cols)
    parts = lax.all_to_all(pack, ("dp", "template"), 0, 0, tiled=True)
    total = jnp.sum(parts, axis=0)
    ratio_block = (
        jnp.zeros((piece, 128), jnp.float32)
        .at[:, 0]
        .set(total[:, 2 * heads] / total[:, 2 * heads + 1])
    )
    done = jnp.concatenate([total[:, :heads] / total[:, heads : 2 * heads], ratio_block], axis=1)
    spread = lax.all_to_all(
        jnp.broadcast_to(done[None], (n_t,) + done.shape), "template", 0, 0, tiled=True
    )
    full = spread.reshape(n_t * piece, done.shape[1])
    merged = full[:, :heads]
    merged_gain = full[:, heads]
    return (merged, merged_gain)


def solution(mesh):
    in_specs = (
        P("template", ("fsdp", "dp"), None),
        P("template", ("fsdp", "dp"), None),
        P("template", "fsdp", None),
        P("template", "fsdp"),
    )
    out_specs = (P(("fsdp", "dp"), None), P(("fsdp", "dp")))
    return jax.shard_map(body, mesh=mesh, in_specs=in_specs, out_specs=out_specs, check_vma=False)
```

profile of v0, /device:TPU:1, one launch (start us, length us, event | category | flops | bytes accessed | tf_op | source)
XLA Modules:
  0.0 301.3 jit_solution(15434402891482876748)
XLA Ops:
  7.2 0.8 fusion.35
  8.0 1.0 dynamic-slice_bitcast_fusion
  9.0 0.7 maximum_bitcast_fusion
  9.7 4.0 %collective-permute-start = (bf16[128,8192]{1,0:T(8,128)(2,1)}, bf16[128,8192]{1,0:T(8,128)(2,1)S(1)}, u32[]{:S(2)}, u32[]{:S(2)}) collective-permute-start(bf16[128,8192]{1,0:T(8,128)(2,1)} %bitcast.50), channel_id=1, source_target_pairs={{0,1},{1,0},{2,3},{3,2},{4,5},{5,4},{6,7},{7,6},{8,9},{9,8},{10,11... | collective-permute-start | bytes 6291464 | tf_op jit(solution)/shard_map/ppermute | solution.py:22
  13.7 2.4 copy.21
  16.1 1.3 copy-done.1
  17.5 2.5 copy.37
  20.0 34.3 %collective-permute-done = bf16[128,8192]{1,0:T(8,128)(2,1)S(1)} collective-permute-done((bf16[128,8192]{1,0:T(8,128)(2,1)}, bf16[128,8192]{1,0:T(8,128)(2,1)S(1)}, u32[]{:S(2)}, u32[]{:S(2)}) %collective-permute-start) | collective-permute-done | bytes 2097184 | tf_op jit(solution)/shard_map/ppermute | solution.py:22
  54.8 31.8 %all-gather.9.cloned.1.call-done = bf16[16,514,256]{2,1,0:T(8,128)(2,1)} async-done(((bf16[1,514,256]{2,1,0:T(8,128)(2,1)}), bf16[16,514,256]{2,1,0:T(8,128)(2,1)}) %all-gather.9.cloned.1.call-update) | async-done | bytes 4210704 | tf_op jit(solution)/shard_map/all_gather | solution.py:29
  86.7 1.0 slice_convert_fusion
  88.9 0.7 fusion.24
  89.6 6.2 %all-to-all-start = ((bf16[16,128,512]{2,1,0:T(8,128)(2,1)}), bf16[16,128,512]{2,1,0:T(8,128)(2,1)}, u32[]{:S(2)}, u32[]{:S(2)}) async-start(bf16[16,128,512]{2,1,0:T(8,128)(2,1)} %bitcast.52), calls=%async_computation | async-start | bytes 4194304 | tf_op jit(solution)/shard_map/all_to_all | solution.py:57
  96.4 3.1 %collective-permute-start.1 = (f32[128,256]{1,0:T(8,128)S(1)}, f32[128,256]{1,0:T(8,128)S(1)}, u32[]{:S(2)}, u32[]{:S(2)}) collective-permute-start(f32[128,256]{1,0:T(8,128)S(1)} %fusion.24), channel_id=1, source_target_pairs={{0,1},{1,0},{2,3},{3,2},{4,5},{5,4},{6,7},{7,6},{8,9},{9,8},{10,11... | collective-permute-start | bytes 393224 | tf_op jit(solution)/shard_map/ppermute | solution.py:48
  99.6 5.5 %fusion.21 = f32[128,256]{1,0:T(8,128)S(1)} fusion(bf16[16,514,256]{2,1,0:T(8,128)(2,1)} %all-gather.9.cloned.1.call-done, f32[16,512]{1,0:T(8,128)S(1)} %bitcast.60, f32[128]{0:T(128)S(1)} %get-tuple-element.49, bf16[128,16,512]{2,1,0:T(8,128)(2,1)} %bitcast.54), kind=kOutput, calls=%fused_computation.29 | convolution fusion | flops 541065216 | bytes 6455808 | tf_op jit(solution)/shard_map/tfr,frh->th/dot_general | solution.py:36
  105.1 0.7 fusion.31
  107.3 111.4 %all-gather.3 = f32[16,1,128]{2,1,0:T(1,128)S(1)} all-gather(f32[1,1,128]{2,1,0:T(1,128)S(1)} %get-tuple-element.48), channel_id=3, replica_groups=mesh['template'=16,'fsdp'=16,'dp'=2] {'fsdp'}, dimensions={0}, use_global_device_ids=true | all-gather | bytes 8704 | tf_op jit(solution)/shard_map/all_gather | solution.py:58
  218.7 2.2 all-gather.7.cloned.1.call-done
  220.9 4.0 %fusion.7 = f32[512]{0:T(512)S(1)} fusion(bf16[2048,512]{1,0:T(8,128)(2,1)} %bitcast.16, bf16[2048,512]{1,0:T(8,128)(2,1)} %all-gather.7.cloned.1.call-done, f32[2048]{0:T(1024)S(1)} %bitcast.61, bf16[1,512,512]{2,1,0:T(8,128)(2,1)S(1)} %copy-done.2), kind=kOutput, calls=%fused_computation.10 | convolution fusion | flops 1080032768 | bytes 4728832 | tf_op jit(solution)/shard_map/th,dh->td/dot_general | solution.py:66
  224.9 1.2 broadcast_select_fusion.2
  226.4 3.3 %convert_multiply_fusion.3 = (f32[512,512]{0,1:T(8,128)S(1)}, f32[512,512]{0,1:T(8,128)S(1)}) fusion(bf16[1,512,512]{1,2,0:T(8,128)(2,1)S(1)} %copy.18, bf16[2048,512]{1,0:T(8,128)(2,1)S(1)} %copy-done.6, bf16[2048,512]{1,0:T(8,128)(2,1)} %bitcast.16, f32[2048]{0:T(1024)S(1)} %bitcast.62, f32[512]{0:T(512)S(1)} %bitcast.63), kind=kOutput, calls=%fused_computation.31 | convolution fusion | flops 1084751872 | bytes 6825984 | tf_op jit(solution)/shard_map/td,th->dh/dot_general | solution.py:65
  229.9 2.0 copy.19
  231.9 43.6 %all_to_all.15 = f32[32,16,1152]{2,1,0:T(8,128)S(1)} all-to-all(f32[32,16,1152]{2,1,0:T(8,128)} %bitcast.49), channel_id=1, replica_groups=mesh['template'=16,'fsdp'=16,'dp'=2] {'dp','template'}, dimensions={0} | all-to-all | bytes 4718592 | tf_op jit(solution)/shard_map/all_to_all | solution.py:74
  276.3 16.6 %all_to_all.16 = f32[16,16,640]{2,1,0:T(8,128)S(1)} all-to-all(f32[16,16,640]{2,1,0:T(8,128)S(1)} %broadcast_in_dim.2), channel_id=1, replica_groups=mesh['template'=16,'fsdp'=16,'dp'=2] {'template'}, dimensions={0} | all-to-all | bytes 1310720 | tf_op jit(solution)/shard_map/all_to_all | solution.py:82
  293.0 0.9 slice.81
  (40 shorter events, 5.8 us)
Async XLA Ops:
  7.2 79.5 %all-gather.9.cloned.1.call-start = ((), (), s32[]{:S(2)}) async-start(), calls=%async_computation.4 | async-start | bytes 4526080 | tf_op jit(solution)/shard_map/all_gather | solution.py:29
  9.7 44.6 %collective-permute-start = (bf16[128,8192]{1,0:T(8,128)(2,1)}, bf16[128,8192]{1,0:T(8,128)(2,1)S(1)}, u32[]{:S(2)}, u32[]{:S(2)}) collective-permute-start(bf16[128,8192]{1,0:T(8,128)(2,1)} %bitcast.50), channel_id=1, source_target_pairs={{0,1},{1,0},{2,3},{3,2},{4,5},{5,4},{6,7},{7,6},{8,9},{9,8},{10,11... | collective-permute-start | bytes 6291464 | tf_op jit(solution)/shard_map/ppermute | solution.py:22
  16.1 1.4 copy-start.1
  86.7 2.2 copy-start.5
  89.6 6.3 %copy-start = (bf16[1,128,8192]{2,1,0:T(8,128)(2,1)S(1)}, bf16[1,128,8192]{2,1,0:T(8,128)(2,1)}, u32[]{:S(2)}) copy-start(bf16[1,128,8192]{2,1,0:T(8,128)(2,1)} %param.10) | copy-start | bytes 6291460
  89.6 131.3 %all-to-all-start = ((bf16[16,128,512]{2,1,0:T(8,128)(2,1)}), bf16[16,128,512]{2,1,0:T(8,128)(2,1)}, u32[]{:S(2)}, u32[]{:S(2)}) async-start(bf16[16,128,512]{2,1,0:T(8,128)(2,1)} %bitcast.52), calls=%async_computation | async-start | bytes 4194304 | tf_op jit(solution)/shard_map/all_to_all | solution.py:57
  95.9 125.0 %all-gather.7.cloned.1.call-start = ((), (), s32[]{:S(2)}) async-start(), calls=%async_computation.3 | async-start | bytes 2228224 | tf_op jit(solution)/shard_map/all_gather | solution.py:59
  96.4 8.6 %collective-permute-start.1 = (f32[128,256]{1,0:T(8,128)S(1)}, f32[128,256]{1,0:T(8,128)S(1)}, u32[]{:S(2)}, u32[]{:S(2)}) collective-permute-start(f32[128,256]{1,0:T(8,128)S(1)} %fusion.24), channel_id=1, source_target_pairs={{0,1},{1,0},{2,3},{3,2},{4,5},{5,4},{6,7},{7,6},{8,9},{9,8},{10,11... | collective-permute-start | bytes 393224 | tf_op jit(solution)/shard_map/ppermute | solution.py:48
  99.6 5.6 %copy-start.3 = (bf16[1,128,512]{2,1,0:T(8,128)(2,1)S(1)}, bf16[1,128,512]{2,1,0:T(8,128)(2,1)}, u32[]{:S(2)}) copy-start(bf16[1,128,512]{2,1,0:T(8,128)(2,1)} %param.11) | copy-start | bytes 393220
  99.6 6.3 %copy-start.2 = (bf16[1,512,512]{2,1,0:T(8,128)(2,1)S(1)}, bf16[1,512,512]{2,1,0:T(8,128)(2,1)}, u32[]{:S(2)}) copy-start(bf16[1,512,512]{2,1,0:T(8,128)(2,1)} %param.12) | copy-start | bytes 1572868
  220.9 4.0 %copy-start.4 = (bf16[1,512]{1,0:T(2,128)(2,1)S(1)}, bf16[1,512]{1,0:T(2,128)(2,1)}, u32[]{:S(2)}) copy-start(bf16[1,512]{1,0:T(2,128)(2,1)} %param.13) | copy-start | bytes 3076
  220.9 5.5 %copy-start.6 = (bf16[2048,512]{1,0:T(8,128)(2,1)S(1)}, bf16[2048,512]{1,0:T(8,128)(2,1)}, u32[]{:S(2)}) copy-start(bf16[2048,512]{1,0:T(8,128)(2,1)} %all-gather.7.cloned.1.call-done) | copy-start | bytes 6291460
Sparse Core Ops, SparseCore 0:
  10.7 75.9 all-gather.8
  106.0 114.8 all-gather.6
where the time goes:
time: 302 us; the launch traced here: 301 us
  blocking collectives  172 us (57%)
  waiting for transfers between devices  68.4 us (23%)
  between operations  14.3 us (5%)
  matrix products  13.4 us (4%)
  starting transfers between devices  13.3 us (4%)
  local copies, waits for them, and re-layouts  12 us (4%)
  other arithmetic  8.25 us (3%)
    all_gather x1, blocking collectives, body(): local_ratio = lax.all_gather(ratio, 'fsdp', axis=0, tiled=True)  111 us
    all_to_all x1, blocking collectives, body(): parts = lax.all_to_all(pack, ('dp', 'template'), 0, 0, tiled=True)  43.6 us
    ppermute x1, waiting for transfers between devices, body(): other_hidden = lax.ppermute(token_batch, 'dp', swap)  34.3 us
    all_gather x1, waiting for transfers between devices, body(): gathered = lax.all_gather(w_ext, 'fsdp', axis=0, tiled=False)  31.8 us
    all_to_all x1, blocking collectives, body(): lax.all_to_all(jnp.broadcast_to(done[None], (n_t,) + done.shape), 'templa...  16.6 us
    all_to_all x1, starting transfers between devices, body(): lax.all_to_all(late_batch, 'fsdp', 0, 0, tiled=True).reshape(-1, rows)  6.22 us
  transfers between devices with their start and end apart: 5, of which 3 were waited for; matrix products, arithmetic and copies ran while one was open for 5% of the time, Pallas kernels for 0%

commit v1 on v0

--- a/solution.py
+++ b/solution.py
@@ -3,6 +3,27 @@
 import jax.numpy as jnp
 from jax import lax
 from jax.sharding import PartitionSpec as P
+
+
+def collect(x, axis, dim):
+    length, here, extent = (lax.axis_size(axis), lax.axis_index(axis), x.shape[dim])
+    forward = [(i, (i + 1) % length) for i in range(length)]
+    backward = [(i, (i - 1) % length) for i in range(length)]
+    filled = jnp.zeros((*x.shape[:dim], length * extent, *x.shape[dim + 1 :]), x.dtype)
+    filled = lax.dynamic_update_slice_in_dim(filled, x, here * extent, axis=dim)
+    from_left = from_right = x
+    halfway = length // 2
+    for step in range(1, halfway + 1):
+        from_left = lax.ppermute(from_left, axis, forward)
+        filled = lax.dynamic_update_slice_in_dim(
+            filled, from_left, (here - step) % length * extent, axis=dim
+        )
+        if step < length - halfway:
+            from_right = lax.ppermute(from_right, axis, backward)
+            filled = lax.dynamic_update_slice_in_dim(
+                filled, from_right, (here + step) % length * extent, axis=dim
+            )
+    return filled
 
 
 def body(hidden, target, weight, gain):
@@ -55,7 +76,7 @@
     by_dest = jnp.transpose(token_batch.reshape(token_batch.shape[0], n_f, rows), (1, 0, 2))
     late_batch, _ = lax.optimization_barrier((by_dest, theirs_half))
     local_hidden = lax.all_to_all(late_batch, "fsdp", 0, 0, tiled=True).reshape(-1, rows)
-    local_ratio = lax.all_gather(ratio, "fsdp", axis=0, tiled=True)
+    local_ratio = collect(ratio, "fsdp", 0)
     local_delta = lax.all_gather(delta, "fsdp", axis=0, tiled=True)
     local_xhat = local_hidden.astype(jnp.float32) * local_ratio
     g_f = g_shard.astype(jnp.float32)

time: 302 us -> 330 us (1.093)
  blocking collectives: 172 us -> 69.5 us
  waiting for transfers between devices: 68.4 us -> 144 us
  starting transfers between devices: 13.3 us -> 64.8 us
    all_gather x1 -> x0, blocking collectives: 111 us -> none  [body(): local_ratio = lax.all_gather(ratio, 'fsdp', axis=0, tiled=True)]
    ppermute x0 -> x15, waiting for transfers between devices: none -> 78.2 us  [the longest x8 76.2 us: collect(): from_left = lax.ppermute(from_left, axis, forward)]
    ppermute x0 -> x15, starting transfers between devices: none -> 51.4 us  [the longest x8 27.7 us: collect(): from_left = lax.ppermute(from_left, axis, forward)]
    all_to_all x1, blocking collectives: 43.6 us -> 52.9 us  [body(): parts = lax.all_to_all(pack, ('dp', 'template'), 0, 0, tiled=True)]
  transfers between devices with their start and end apart: 5 -> 20, of which waited for: 3 -> 5; matrix products, arithmetic and copies ran while one was open for 5% -> 5% of each run, Pallas kernels for 0% -> 0%
where the time goes in v1:
time: 330 us; the launch traced here: 329 us
  waiting for transfers between devices  144 us (44%)
  blocking collectives  69.5 us (21%)
  starting transfers between devices  64.8 us (20%)
  between operations  14.8 us (4%)
  local copies, waits for them, and re-layouts  13.4 us (4%)
  matrix products  13.4 us (4%)
  other arithmetic  8.78 us (3%)
    ppermute x8, waiting for transfers between devices, collect(): from_left = lax.ppermute(from_left, axis, forward)  76.2 us
    all_to_all x1, blocking collectives, body(): parts = lax.all_to_all(pack, ('dp', 'template'), 0, 0, tiled=True)  52.9 us
    ppermute x1, waiting for transfers between devices, body(): other_hidden = lax.ppermute(token_batch, 'dp', swap)  34.3 us
    all_gather x1, waiting for transfers between devices, body(): gathered = lax.all_gather(w_ext, 'fsdp', axis=0, tiled=False)  31.8 us
    ppermute x8, starting transfers between devices, collect(): from_left = lax.ppermute(from_left, axis, forward)  27.7 us
    ppermute x7, starting transfers between devices, collect(): from_right = lax.ppermute(from_right, axis, backward)  23.7 us
    all_to_all x1, blocking collectives, body(): lax.all_to_all(jnp.broadcast_to(done[None], (n_t,) + done.shape), 'templa...  16.6 us
  transfers between devices with their start and end apart: 20, of which 5 were waited for; matrix products, arithmetic and copies ran while one was open for 5% of the time, Pallas kernels for 0%

profile of v1, /device:TPU:1, one launch (start us, length us, event | category | flops | bytes accessed | tf_op | source)
XLA Modules:
  0.0 329.2 jit_solution(7894327605468258051)
XLA Ops:
  9.7 4.0 %collective-permute-start = (bf16[128,8192]{1,0:T(8,128)(2,1)}, bf16[128,8192]{1,0:T(8,128)(2,1)S(1)}, u32[]{:S(2)}, u32[]{:S(2)}) collective-permute-start(bf16[128,8192]{1,0:T(8,128)(2,1)} %bitcast.79), channel_id=1, source_target_pairs={{0,1},{1,0},{2,3},{3,2},{4,5},{5,4},{6,7},{7,6},{8,9},{9,8},{10,11... | collective-permute-start | bytes 6291464 | tf_op jit(solution)/shard_map/ppermute | solution.py:43
  13.7 2.4 copy.21
  17.5 2.5 copy.37
  20.0 34.3 %collective-permute-done = bf16[128,8192]{1,0:T(8,128)(2,1)S(1)} collective-permute-done((bf16[128,8192]{1,0:T(8,128)(2,1)}, bf16[128,8192]{1,0:T(8,128)(2,1)S(1)}, u32[]{:S(2)}, u32[]{:S(2)}) %collective-permute-start) | collective-permute-done | bytes 2097184 | tf_op jit(solution)/shard_map/ppermute | solution.py:43
  54.8 31.8 %all-gather.7.cloned.1.call-done = bf16[16,514,256]{2,1,0:T(8,128)(2,1)} async-done(((bf16[1,514,256]{2,1,0:T(8,128)(2,1)}), bf16[16,514,256]{2,1,0:T(8,128)(2,1)}) %all-gather.7.cloned.1.call-update) | async-done | bytes 4210704 | tf_op jit(solution)/shard_map/all_gather | solution.py:50
  89.6 6.2 %all-to-all-start = ((bf16[16,128,512]{2,1,0:T(8,128)(2,1)}), bf16[16,128,512]{2,1,0:T(8,128)(2,1)}, u32[]{:S(2)}, u32[]{:S(2)}) async-start(bf16[16,128,512]{2,1,0:T(8,128)(2,1)} %bitcast.81), calls=%async_computation | async-start | bytes 4194304 | tf_op jit(solution)/shard_map/all_to_all | solution.py:78
  96.6 3.1 collective-permute-start.16
  99.7 5.5 %fusion.21 = f32[128,256]{1,0:T(8,128)S(1)} fusion(bf16[16,514,256]{2,1,0:T(8,128)(2,1)} %all-gather.7.cloned.1.call-done, f32[16,512]{1,0:T(8,128)S(1)} %bitcast.89, f32[128]{0:T(128)S(1)} %get-tuple-element.50, bf16[128,16,512]{2,1,0:T(8,128)(2,1)} %bitcast.83), kind=kOutput, calls=%fused_computation.29 | convolution fusion | flops 541065216 | bytes 6455808 | tf_op jit(solution)/shard_map/tfr,frh->th/dot_general | solution.py:57
  106.0 3.2 collective-permute-start.1
  109.2 3.3 collective-permute-start.2
  114.4 72.9 %collective-permute-done.1 = f32[128,1]{0,1:T(1,128)S(1)} collective-permute-done((f32[128,1]{0,1:T(1,128)S(1)}, f32[128,1]{0,1:T(1,128)S(1)}, u32[]{:S(2)}, u32[]{:S(2)}) %collective-permute-start.1) | collective-permute-done | bytes 544 | tf_op jit(solution)/shard_map/ppermute | solution.py:17
  187.2 8.4 %collective-permute-start.3 = (f32[128,1]{0,1:T(1,128)S(1)}, f32[128,1]{0,1:T(1,128)S(1)}, u32[]{:S(2)}, u32[]{:S(2)}) collective-permute-start(f32[128,1]{0,1:T(1,128)S(1)} %collective-permute-done.1), channel_id=1, source_target_pairs={{0,2},{2,4},{4,6},{6,8},{8,10},{10,12},{12,14},{14,16},{16,18},{18... | collective-permute-start | bytes 1544 | tf_op jit(solution)/shard_map/ppermute | solution.py:17
  199.7 4.9 %collective-permute-start.5 = (f32[128,1]{0,1:T(1,128)S(1)}, f32[128,1]{0,1:T(1,128)S(1)}, u32[]{:S(2)}, u32[]{:S(2)}) collective-permute-start(f32[128,1]{0,1:T(1,128)S(1)} %collective-permute-done.3), channel_id=1, source_target_pairs={{0,2},{2,4},{4,6},{6,8},{8,10},{10,12},{12,14},{14,16},{16,18},{18... | collective-permute-start | bytes 1544 | tf_op jit(solution)/shard_map/ppermute | solution.py:17
  206.8 3.4 %collective-permute-start.7 = (f32[128,1]{0,1:T(1,128)S(1)}, f32[128,1]{0,1:T(1,128)S(1)}, u32[]{:S(2)}, u32[]{:S(2)}) collective-permute-start(f32[128,1]{0,1:T(1,128)S(1)} %collective-permute-done.5), channel_id=1, source_target_pairs={{0,2},{2,4},{4,6},{6,8},{8,10},{10,12},{12,14},{14,16},{16,18},{18... | collective-permute-start | bytes 1544 | tf_op jit(solution)/shard_map/ppermute | solution.py:17
  210.1 3.1 collective-permute-start.8
  213.5 2.1 collective-permute-start.9
  215.6 4.3 %collective-permute-start.10 = (f32[128,1]{0,1:T(1,128)S(1)}, f32[128,1]{0,1:T(1,128)S(1)}, u32[]{:S(2)}, u32[]{:S(2)}) collective-permute-start(f32[128,1]{0,1:T(1,128)S(1)} %collective-permute-done.8), channel_id=1, source_target_pairs={{0,30},{2,0},{4,2},{6,4},{8,6},{10,8},{12,10},{14,12},{16,14},{18,... | collective-permute-start | bytes 1544 | tf_op jit(solution)/shard_map/ppermute | solution.py:22
  222.1 4.6 %collective-permute-start.12 = (f32[128,1]{0,1:T(1,128)S(1)}, f32[128,1]{0,1:T(1,128)S(1)}, u32[]{:S(2)}, u32[]{:S(2)}) collective-permute-start(f32[128,1]{0,1:T(1,128)S(1)} %collective-permute-done.10), channel_id=1, source_target_pairs={{0,30},{2,0},{4,2},{6,4},{8,6},{10,8},{12,10},{14,12},{16,14},{18,... | collective-permute-start | bytes 1544 | tf_op jit(solution)/shard_map/ppermute | solution.py:22
  228.8 4.6 %collective-permute-start.14 = (f32[128,1]{0,1:T(1,128)S(1)}, f32[128,1]{0,1:T(1,128)S(1)}, u32[]{:S(2)}, u32[]{:S(2)}) collective-permute-start(f32[128,1]{0,1:T(1,128)S(1)} %collective-permute-done.12), channel_id=1, source_target_pairs={{0,30},{2,0},{4,2},{6,4},{8,6},{10,8},{12,10},{14,12},{16,14},{18,... | collective-permute-start | bytes 1544 | tf_op jit(solution)/shard_map/ppermute | solution.py:22
  235.8 3.4 %collective-permute-done.15 = f32[128,1]{0,1:T(1,128)S(1)} collective-permute-done((f32[128,1]{0,1:T(1,128)S(1)}, f32[128,1]{0,1:T(1,128)S(1)}, u32[]{:S(2)}, u32[]{:S(2)}) %collective-permute-start.15) | collective-permute-done | bytes 544 | tf_op jit(solution)/shard_map/ppermute | solution.py:17
  239.4 4.0 %fusion.7 = f32[512]{0:T(512)S(1)} fusion(bf16[2048,512]{1,0:T(8,128)(2,1)} %bitcast.30, bf16[2048,512]{1,0:T(8,128)(2,1)} %all-gather.5.cloned.1.call-done, f32[2048]{0:T(1024)S(1)} %bitcast_dynamic-update-slice_fusion, bf16[1,512,512]{2,1,0:T(8,128)(2,1)S(1)} %copy-done.2), kind=kOutput, calls=%fused_computation.10 | convolution fusion | flops 1080032768 | bytes 4728832 | tf_op jit(solution)/shard_map/th,dh->td/dot_general | solution.py:87
  244.8 3.3 convert_multiply_fusion.3
  250.3 52.9 %all_to_all.15 = f32[32,16,1152]{2,1,0:T(8,128)S(1)} all-to-all(f32[32,16,1152]{2,1,0:T(8,128)} %bitcast.78), channel_id=1, replica_groups=mesh['template'=16,'fsdp'=16,'dp'=2] {'dp','template'}, dimensions={0} | all-to-all | bytes 4718592 | tf_op jit(solution)/shard_map/all_to_all | solution.py:95
  304.2 16.6 %all_to_all.16 = f32[16,16,640]{2,1,0:T(8,128)S(1)} all-to-all(f32[16,16,640]{2,1,0:T(8,128)S(1)} %broadcast_in_dim.2), channel_id=1, replica_groups=mesh['template'=16,'fsdp'=16,'dp'=2] {'template'}, dimensions={0} | all-to-all | bytes 1310720 | tf_op jit(solution)/shard_map/all_to_all | solution.py:103
  (85 shorter events, 29.6 us)
Async XLA Ops:
  7.2 79.5 %all-gather.7.cloned.1.call-start = ((), (), s32[]{:S(2)}) async-start(), calls=%async_computation.4 | async-start | bytes 4526080 | tf_op jit(solution)/shard_map/all_gather | solution.py:50
  9.7 44.6 %collective-permute-start = (bf16[128,8192]{1,0:T(8,128)(2,1)}, bf16[128,8192]{1,0:T(8,128)(2,1)S(1)}, u32[]{:S(2)}, u32[]{:S(2)}) collective-permute-start(bf16[128,8192]{1,0:T(8,128)(2,1)} %bitcast.79), channel_id=1, source_target_pairs={{0,1},{1,0},{2,3},{3,2},{4,5},{5,4},{6,7},{7,6},{8,9},{9,8},{10,11... | collective-permute-start | bytes 6291464 | tf_op jit(solution)/shard_map/ppermute | solution.py:43
  89.6 6.3 %copy-start = (bf16[1,128,8192]{2,1,0:T(8,128)(2,1)S(1)}, bf16[1,128,8192]{2,1,0:T(8,128)(2,1)}, u32[]{:S(2)}) copy-start(bf16[1,128,8192]{2,1,0:T(8,128)(2,1)} %param.10) | copy-start | bytes 6291460
  89.6 149.7 %all-to-all-start = ((bf16[16,128,512]{2,1,0:T(8,128)(2,1)}), bf16[16,128,512]{2,1,0:T(8,128)(2,1)}, u32[]{:S(2)}, u32[]{:S(2)}) async-start(bf16[16,128,512]{2,1,0:T(8,128)(2,1)} %bitcast.81), calls=%async_computation | async-start | bytes 4194304 | tf_op jit(solution)/shard_map/all_to_all | solution.py:78
  95.9 143.5 %all-gather.5.cloned.1.call-start = ((), (), s32[]{:S(2)}) async-start(), calls=%async_computation.3 | async-start | bytes 2228224 | tf_op jit(solution)/shard_map/all_gather | solution.py:80
  96.6 8.6 %collective-permute-start.16 = (f32[128,256]{1,0:T(8,128)S(1)}, f32[128,256]{1,0:T(8,128)S(1)}, u32[]{:S(2)}, u32[]{:S(2)}) collective-permute-start(f32[128,256]{1,0:T(8,128)S(1)} %fusion.24), channel_id=1, source_target_pairs={{0,1},{1,0},{2,3},{3,2},{4,5},{5,4},{6,7},{7,6},{8,9},{9,8},{10,11... | collective-permute-start | bytes 393224 | tf_op jit(solution)/shard_map/ppermute | solution.py:69
  99.7 5.6 %copy-start.3 = (bf16[1,128,512]{2,1,0:T(8,128)(2,1)S(1)}, bf16[1,128,512]{2,1,0:T(8,128)(2,1)}, u32[]{:S(2)}) copy-start(bf16[1,128,512]{2,1,0:T(8,128)(2,1)} %param.11) | copy-start | bytes 393220
  99.7 13.0 %copy-start.2 = (bf16[1,512,512]{2,1,0:T(8,128)(2,1)S(1)}, bf16[1,512,512]{2,1,0:T(8,128)(2,1)}, u32[]{:S(2)}) copy-start(bf16[1,512,512]{2,1,0:T(8,128)(2,1)} %param.12) | copy-start | bytes 1572868
  106.0 81.3 %collective-permute-start.1 = (f32[128,1]{0,1:T(1,128)S(1)}, f32[128,1]{0,1:T(1,128)S(1)}, u32[]{:S(2)}, u32[]{:S(2)}) collective-permute-start(f32[128,1]{0,1:T(1,128)S(1)} %get-tuple-element.48), channel_id=1, source_target_pairs={{0,2},{2,4},{4,6},{6,8},{8,10},{10,12},{12,14},{14,16},{16,18},{18... | collective-permute-start | bytes 1544 | tf_op jit(solution)/shard_map/ppermute | solution.py:17
  109.2 88.4 %collective-permute-start.2 = (f32[128,1]{0,1:T(1,128)S(1)}, f32[128,1]{0,1:T(1,128)S(1)}, u32[]{:S(2)}, u32[]{:S(2)}) collective-permute-start(f32[128,1]{0,1:T(1,128)S(1)} %get-tuple-element.48), channel_id=1, source_target_pairs={{0,30},{2,0},{4,2},{6,4},{8,6},{10,8},{12,10},{14,12},{16,14},{18,... | collective-permute-start | bytes 1544 | tf_op jit(solution)/shard_map/ppermute | solution.py:22
  187.2 12.5 %collective-permute-start.3 = (f32[128,1]{0,1:T(1,128)S(1)}, f32[128,1]{0,1:T(1,128)S(1)}, u32[]{:S(2)}, u32[]{:S(2)}) collective-permute-start(f32[128,1]{0,1:T(1,128)S(1)} %collective-permute-done.1), channel_id=1, source_target_pairs={{0,2},{2,4},{4,6},{6,8},{8,10},{10,12},{12,14},{14,16},{16,18},{18... | collective-permute-start | bytes 1544 | tf_op jit(solution)/shard_map/ppermute | solution.py:17
  197.6 7.0 %collective-permute-start.4 = (f32[128,1]{0,1:T(1,128)S(1)}, f32[128,1]{0,1:T(1,128)S(1)}, u32[]{:S(2)}, u32[]{:S(2)}) collective-permute-start(f32[128,1]{0,1:T(1,128)S(1)} %collective-permute-done.2), channel_id=1, source_target_pairs={{0,30},{2,0},{4,2},{6,4},{8,6},{10,8},{12,10},{14,12},{16,14},{18,... | collective-permute-start | bytes 1544 | tf_op jit(solution)/shard_map/ppermute | solution.py:22
  199.7 7.0 %collective-permute-start.5 = (f32[128,1]{0,1:T(1,128)S(1)}, f32[128,1]{0,1:T(1,128)S(1)}, u32[]{:S(2)}, u32[]{:S(2)}) collective-permute-start(f32[128,1]{0,1:T(1,128)S(1)} %collective-permute-done.3), channel_id=1, source_target_pairs={{0,2},{2,4},{4,6},{6,8},{8,10},{10,12},{12,14},{14,16},{16,18},{18... | collective-permute-start | bytes 1544 | tf_op jit(solution)/shard_map/ppermute | solution.py:17
  204.6 5.5 %collective-permute-start.6 = (f32[128,1]{0,1:T(1,128)S(1)}, f32[128,1]{0,1:T(1,128)S(1)}, u32[]{:S(2)}, u32[]{:S(2)}) collective-permute-start(f32[128,1]{0,1:T(1,128)S(1)} %collective-permute-done.4), channel_id=1, source_target_pairs={{0,30},{2,0},{4,2},{6,4},{8,6},{10,8},{12,10},{14,12},{16,14},{18,... | collective-permute-start | bytes 1544 | tf_op jit(solution)/shard_map/ppermute | solution.py:22
  206.8 6.7 %collective-permute-start.7 = (f32[128,1]{0,1:T(1,128)S(1)}, f32[128,1]{0,1:T(1,128)S(1)}, u32[]{:S(2)}, u32[]{:S(2)}) collective-permute-start(f32[128,1]{0,1:T(1,128)S(1)} %collective-permute-done.5), channel_id=1, source_target_pairs={{0,2},{2,4},{4,6},{6,8},{8,10},{10,12},{12,14},{14,16},{16,18},{18... | collective-permute-start | bytes 1544 | tf_op jit(solution)/shard_map/ppermute | solution.py:17
  210.1 5.5 %collective-permute-start.8 = (f32[128,1]{0,1:T(1,128)S(1)}, f32[128,1]{0,1:T(1,128)S(1)}, u32[]{:S(2)}, u32[]{:S(2)}) collective-permute-start(f32[128,1]{0,1:T(1,128)S(1)} %collective-permute-done.6), channel_id=1, source_target_pairs={{0,30},{2,0},{4,2},{6,4},{8,6},{10,8},{12,10},{14,12},{16,14},{18,... | collective-permute-start | bytes 1544 | tf_op jit(solution)/shard_map/ppermute | solution.py:22
  213.5 6.7 %collective-permute-start.9 = (f32[128,1]{0,1:T(1,128)S(1)}, f32[128,1]{0,1:T(1,128)S(1)}, u32[]{:S(2)}, u32[]{:S(2)}) collective-permute-start(f32[128,1]{0,1:T(1,128)S(1)} %collective-permute-done.7), channel_id=1, source_target_pairs={{0,2},{2,4},{4,6},{6,8},{8,10},{10,12},{12,14},{14,16},{16,18},{18... | collective-permute-start | bytes 1544 | tf_op jit(solution)/shard_map/ppermute | solution.py:17
  215.6 6.5 %collective-permute-start.10 = (f32[128,1]{0,1:T(1,128)S(1)}, f32[128,1]{0,1:T(1,128)S(1)}, u32[]{:S(2)}, u32[]{:S(2)}) collective-permute-start(f32[128,1]{0,1:T(1,128)S(1)} %collective-permute-done.8), channel_id=1, source_target_pairs={{0,30},{2,0},{4,2},{6,4},{8,6},{10,8},{12,10},{14,12},{16,14},{18,... | collective-permute-start | bytes 1544 | tf_op jit(solution)/shard_map/ppermute | solution.py:22
  220.2 6.7 %collective-permute-start.11 = (f32[128,1]{0,1:T(1,128)S(1)}, f32[128,1]{0,1:T(1,128)S(1)}, u32[]{:S(2)}, u32[]{:S(2)}) collective-permute-start(f32[128,1]{0,1:T(1,128)S(1)} %collective-permute-done.9), channel_id=1, source_target_pairs={{0,2},{2,4},{4,6},{6,8},{8,10},{10,12},{12,14},{14,16},{16,18},{18... | collective-permute-start | bytes 1544 | tf_op jit(solution)/shard_map/ppermute | solution.py:17
  222.1 6.7 %collective-permute-start.12 = (f32[128,1]{0,1:T(1,128)S(1)}, f32[128,1]{0,1:T(1,128)S(1)}, u32[]{:S(2)}, u32[]{:S(2)}) collective-permute-start(f32[128,1]{0,1:T(1,128)S(1)} %collective-permute-done.10), channel_id=1, source_target_pairs={{0,30},{2,0},{4,2},{6,4},{8,6},{10,8},{12,10},{14,12},{16,14},{18,... | collective-permute-start | bytes 1544 | tf_op jit(solution)/shard_map/ppermute | solution.py:22
  226.9 6.7 %collective-permute-start.13 = (f32[128,1]{0,1:T(1,128)S(1)}, f32[128,1]{0,1:T(1,128)S(1)}, u32[]{:S(2)}, u32[]{:S(2)}) collective-permute-start(f32[128,1]{0,1:T(1,128)S(1)} %collective-permute-done.11), channel_id=1, source_target_pairs={{0,2},{2,4},{4,6},{6,8},{8,10},{10,12},{12,14},{14,16},{16,18},{18... | collective-permute-start | bytes 1544 | tf_op jit(solution)/shard_map/ppermute | solution.py:17
  228.8 6.8 %collective-permute-start.14 = (f32[128,1]{0,1:T(1,128)S(1)}, f32[128,1]{0,1:T(1,128)S(1)}, u32[]{:S(2)}, u32[]{:S(2)}) collective-permute-start(f32[128,1]{0,1:T(1,128)S(1)} %collective-permute-done.12), channel_id=1, source_target_pairs={{0,30},{2,0},{4,2},{6,4},{8,6},{10,8},{12,10},{14,12},{16,14},{18,... | collective-permute-start | bytes 1544 | tf_op jit(solution)/shard_map/ppermute | solution.py:22
  233.6 5.5 %collective-permute-start.15 = (f32[128,1]{0,1:T(1,128)S(1)}, f32[128,1]{0,1:T(1,128)S(1)}, u32[]{:S(2)}, u32[]{:S(2)}) collective-permute-start(f32[128,1]{0,1:T(1,128)S(1)} %collective-permute-done.13), channel_id=1, source_target_pairs={{0,2},{2,4},{4,6},{6,8},{8,10},{10,12},{12,14},{14,16},{16,18},{18... | collective-permute-start | bytes 1544 | tf_op jit(solution)/shard_map/ppermute | solution.py:17
  239.4 5.4 %copy-start.6 = (bf16[2048,512]{1,0:T(8,128)(2,1)S(1)}, bf16[2048,512]{1,0:T(8,128)(2,1)}, u32[]{:S(2)}) copy-start(bf16[2048,512]{1,0:T(8,128)(2,1)} %all-gather.5.cloned.1.call-done) | copy-start | bytes 6291460
  (3 other events, 7.6 us)
Sparse Core Ops, SparseCore 0:
  10.7 75.9 all-gather.6
  106.1 114.1 all-gather.4
